TPU v7x, 32 devices: a whole 2x2x4 slice. The times are simulated.
32 devices in a mesh: grp: 2 (over y), row: 4 (over z), col: 2 (over x), sub: 2 (over core).
Axes of the slice: x: 2, y: 2, z: 4, core: 2. Of those that a mesh axis runs over, the one named last changes fastest.
Arguments:
- a_blocks: bfloat16 [16, 2, 4, 2, 256, 256], P(('grp', 'row', 'sub'), 'col'), parts along dimension 0, may hold values from 20 to 2000
- block_list: int32 [16, 2, 4, 2], P(('grp', 'row', 'sub'), 'col'), parts along dimension 0, may hold values from 0 to 3, as said below
- block_count: int32 [16, 2, 4], P(('grp', 'row', 'sub'), 'col'), parts along dimension 0, may hold values from 1 to 2
- w_factor: bfloat16 [16, 1024, 256], P(('grp', 'row', 'sub')), parts along dimension 0, may hold values from 0.05 to 4
- h_factor: bfloat16 [256, 4096], P(None, ('grp', 'row', 'col')), parts along dimension 1, may hold values from 0.05 to 4
Outputs:
- w_new: float32 [16, 1024, 256], P(('grp', 'row', 'sub'), 'col'), parts along dimension 0
- h_new: float32 [256, 4096], P(None, ('grp', 'row', 'col')), parts along dimension 1
There are 2 independent parts, one for each index of `grp`. A program takes and returns all parts, laid end to end along the dimension named above; each array names one. Nothing has to cross between parts.
Inputs may be any that keep to these rules, and one draw needn't show every extreme that they name: `block_list`: within one block row and column group the 2 slots name different column blocks.
All inputs are finite; a program needn't handle non-finite values.
Results may differ from a plain program's by a relative error of at most 0.0003.
Values may be sent and summed in bfloat16 or wider, within the bound.
No kernel may reach another device: no remote copies, remote signals or barrier semaphores. Data moves between devices by JAX's collectives and lax.ppermute only.
A program may use at most 64 MiB of HBM per device.

v0:
```python
import jax
import jax.numpy as jnp
from jax import lax
from jax.sharding import PartitionSpec as P


def body(a_blocks, block_list, block_count, w_factor, h_factor):
    values = a_blocks[0, 0]
    lists = block_list[0, 0]
    counts = block_count[0, 0]
    w_tile = w_factor[0]
    row_blocks, stored, width = (values.shape[0], values.shape[1], values.shape[2])
    rank = w_tile.shape[1]
    tile_rows = w_tile.shape[0]
    n_row = lax.axis_size("row")
    w_rows = w_tile.reshape(row_blocks, width, rank)
    h_all = lax.all_gather(h_factor, "row", axis=1, tiled=True)
    numer_h = jnp.zeros((rank, n_row * width), jnp.float32)
    parts_w = []
    for brow in range(row_blocks):
        part_w = jnp.zeros((width, rank), jnp.float32)
        for slot in range(stored):
            target = lists[brow, slot]
            live = slot < counts[brow]
            h_block = lax.dynamic_slice_in_dim(h_all, target * width, width, 1)
            product = jnp.dot(w_rows[brow], h_block, preferred_element_type=jnp.float32)
            ratios = (values[brow, slot].astype(jnp.float32) / product).astype(jnp.bfloat16)
            ratios = jnp.where(live, ratios, jnp.zeros_like(ratios))
            part_h = jnp.einsum(
                "ik,ij->kj", w_rows[brow], ratios, preferred_element_type=jnp.float32
            )
            part_w = part_w + jnp.einsum(
                "ij,kj->ik", ratios, h_block, preferred_element_type=jnp.float32
            )
            old = lax.dynamic_slice_in_dim(numer_h, target * width, width, 1)
            numer_h = lax.dynamic_update_slice_in_dim(numer_h, old + part_h, target * width, 1)
        parts_w.append(part_w)
    numer_w = jnp.stack(parts_w).reshape(tile_rows, rank)
    col_first = lax.axis_index("col") == 0
    sub_first = lax.axis_index("sub") == 0
    w_sum = jnp.sum(w_tile.astype(jnp.float32), axis=0)
    h_sum = jnp.sum(h_factor.astype(jnp.float32), axis=1)
    sums = jnp.concatenate([jnp.where(col_first, w_sum, 0.0), jnp.where(sub_first, h_sum, 0.0)])
    sums = lax.psum(sums, ("row", "col", "sub"))
    w_total = sums[:rank]
    h_total = sums[rank:]
    numer_h = lax.psum_scatter(numer_h, "row", scatter_dimension=1, tiled=True)
    numer_h = lax.psum(numer_h, "sub")
    h_new = h_factor.astype(jnp.float32) * numer_h / w_total[:, None]
    share = tile_rows // lax.axis_size("col")
    col_index = lax.axis_index("col")
    mine = lax.psum_scatter(numer_w, "col", scatter_dimension=0, tiled=True)
    w_part = lax.dynamic_slice_in_dim(w_tile, col_index * share, share, 0).astype(jnp.float32)
    w_new = (w_part * mine / h_total[None, :])[None]
    return (w_new, h_new)


def solution(mesh):
    placed = (
        P(("grp", "row", "sub"), "col", None, None, None, None),
        P(("grp", "row", "sub"), "col", None, None),
        P(("grp", "row", "sub"), "col", None),
        P(("grp", "row", "sub"), None, None),
        P(None, ("grp", "row", "col")),
    )
    return jax.shard_map(
        body,
        mesh=mesh,
        in_specs=placed,
        out_specs=(P(("grp", "row", "sub"), "col", None), P(None, ("grp", "row", "col"))),
        check_vma=False,
    )
```

profile of v0, /device:TPU:0, one launch (start us, length us, event | category | flops | bytes accessed | tf_op | source)
XLA Modules:
  0.0 123.8 jit_solution(1494217705936552093)
XLA Ops:
  7.2 0.0 reduce-scatter.5.cloned.1.call-start
  7.2 1.5 %fusion.116 = (s32[1,1,1]{2,1,0:T(1,128)}, s32[1,1,1]{2,1,0:T(1,128)}, s32[1,1,1]{2,1,0:T(1,128)}, s32[1,1,1]{2,1,0:T(1,128)}) fusion(s32[1,1,4]{2,1,0:T(1,128)} %param.7), kind=kLoop, calls=%fused_computation.152 | loop fusion | bytes 32 | tf_op jit(solution)/shard_map/slice | solution.py:24
  13.8 0.0 copy-start.3
  13.8 0.7 copy-done.3
  14.5 0.7 fusion.115
  20.1 17.6 %all_gather.3 = bf16[256,1024]{1,0:T(8,128)(2,1)S(1)} all-gather(bf16[256,256]{1,0:T(8,128)(2,1)} %param.9), channel_id=1, replica_groups=mesh['grp'=2,'row'=4,'col'=2,'sub'=2] {'row'}, dimensions={1}, use_global_device_ids=true | all-gather | bytes 655360 | tf_op jit(solution)/shard_map/all_gather | solution.py:17
  37.7 0.0 copy-start.1
  37.7 1.5 %copy.7 = bf16[1,1,4,2,256,256]{4,5,3,2,1,0:T(8,128)(2,1)S(1)} copy(bf16[1,1,4,2,256,256]{5,4,3,2,1,0:T(8,128)(2,1)} %param.5) | data formatting | bytes 2097152 | tf_op args[0]
  39.3 0.0 copy-done.1
  39.3 0.3 fusion.35
  39.5 0.3 fusion.36
  39.8 0.2 fusion.37
  40.0 0.2 fusion.38
  40.3 0.3 fusion.39
  40.6 0.2 fusion.40
  40.8 0.3 fusion.41
  41.1 0.2 fusion.42
  41.3 0.1 broadcast_in_dim.15
  41.4 0.2 fusion.18
  41.6 0.2 fusion.17
  41.8 0.2 fusion.15
  42.0 0.2 fusion.13
  42.2 0.2 fusion.11
  42.4 0.2 fusion.9
  42.6 0.2 fusion.7
  42.8 0.2 fusion.5
  43.0 0.0 copy-start
  43.0 1.0 copy-done
  44.0 0.0 reduce-scatter.5.cloned.1.call-update
  44.1 0.0 reduce-scatter.3.cloned.1.call-start
  44.1 0.2 fusion.79
  44.3 0.2 fusion.3
  44.6 0.2 fusion.74
  44.8 0.2 fusion.2
  45.1 0.2 fusion.69
  45.3 0.2 fusion.1
  45.5 0.2 fusion.64
  45.8 0.2 fusion
  46.0 1.1 pad_maximum_fusion
  47.1 0.0 copy-start.2
  47.1 0.0 reduce-scatter.3.cloned.1.call-update
  47.1 0.0 all-reduce.2.cloned.1.call-start
  47.1 0.8 copy-done.2
  48.0 0.1 copy.8
  48.1 0.1 convert_reduce_fusion.1
  48.1 0.2 convert_reduce_fusion
  48.3 30.9 %psum.14 = f32[512]{0:T(512)S(1)} all-reduce(f32[512]{0:T(512)S(1)} %pad_maximum_fusion.1), channel_id=1, replica_groups=mesh['grp'=2,'row'=4,'col'=2,'sub'=2] {'row','col','sub'}, use_global_device_ids=true, to_apply=%region_3.4 | all-reduce | flops 512 | bytes 4096 | tf_op jit(solution)/shard_map/psum | solution.py:44
  79.2 0.0 reduce-scatter.5.cloned.1.call-done
  79.3 0.0 all-reduce.2.cloned.1.call-update
  79.3 15.5 %reduce-scatter.3.cloned.1.call-done = f32[512,256]{1,0:T(8,128)} async-done(((f32[1024,256]{1,0:T(8,128)}), f32[512,256]{1,0:T(8,128)}) %reduce-scatter.3.cloned.1.call-update) | async-done | bytes 524304 | tf_op jit(solution)/shard_map/reduce_scatter | solution.py:52
  94.8 1.9 %fusion.44 = f32[1,512,256]{2,1,0:T(8,128)} fusion(f32[512,256]{1,0:T(8,128)} %reduce-scatter.3.cloned.1.call-done, f32[256]{0:T(256)S(1)} %get-tuple-element.5, bf16[1,1024,256]{2,1,0:T(8,128)(2,1)S(1)} %copy-done.1, s32[]{:T(128)S(6)} %select_n.106), kind=kLoop, calls=%fused_computation.67 | loop fusion | flops 393216 | bytes 1311748 | tf_op jit(solution)/shard_map/broadcast_in_dim | solution.py:54
  96.7 18.7 %all-reduce.2.cloned.1.call-done = f32[256,256]{0,1:T(8,128)} async-done(((f32[256,256]{0,1:T(8,128)}), f32[256,256]{0,1:T(8,128)}) %all-reduce.2.cloned.1.call-update) | async-done | bytes 262160 | tf_op jit(solution)/shard_map/psum | solution.py:48
  115.4 1.0 fusion.45
  116.4 0.8 copy.9
  (4 shorter events, 0.0 us)
Async XLA Ops:
  7.2 72.1 %reduce-scatter.5.cloned.1.call-start = ((), (), s32[]{:S(2)}) async-start(), calls=%async_computation.3 | async-start | bytes 1310720 | tf_op jit(solution)/shard_map/reduce_scatter | solution.py:47
  13.8 0.7 copy-start.3
  37.7 1.6 %copy-start.1 = (bf16[1,1024,256]{2,1,0:T(8,128)(2,1)S(1)}, bf16[1,1024,256]{2,1,0:T(8,128)(2,1)}, u32[]{:S(2)}) copy-start(bf16[1,1024,256]{2,1,0:T(8,128)(2,1)} %param.8) | copy-start | bytes 1572868
  43.0 1.0 copy-start
  44.1 50.7 %reduce-scatter.3.cloned.1.call-start = ((), (), s32[]{:S(2)}) async-start(), calls=%async_computation.2 | async-start | bytes 1572864 | tf_op jit(solution)/shard_map/reduce_scatter | solution.py:52
  47.1 0.9 copy-start.2
  47.1 68.3 %all-reduce.2.cloned.1.call-start = ((), (), s32[]{:S(2)}) async-start(), calls=%async_computation.4 | async-start | bytes 524288 | tf_op jit(solution)/shard_map/psum | solution.py:48
Sparse Core Ops, SparseCore 0:
  44.2 29.1 reduce-scatter.4
  75.7 18.9 reduce-scatter.2
  97.1 18.2 all-reduce.1
where the time goes:
time: 124 us
  blocking collectives  48.5 us (39%)
  waiting for transfers between devices  34.3 us (28%)
  between operations  24.2 us (20%)
  local copies, waits for them, and re-layouts  7.19 us (6%)
  matrix products  5.36 us (4%)
  other arithmetic  4.15 us (3%)
    psum x1, blocking collectives, body(): sums = lax.psum(sums, ('row', 'col', 'sub'))  30.9 us
    psum x1, waiting for transfers between devices, body(): numer_h = lax.psum(numer_h, 'sub')  18.7 us
    all_gather x1, blocking collectives, body(): h_all = lax.all_gather(h_factor, 'row', axis=1, tiled=True)  17.6 us
    reduce_scatter x1, waiting for transfers between devices, body(): mine = lax.psum_scatter(numer_w, 'col', scatter_dimension=0, tiled=True)  15.5 us
    unnamed x11, local copies, waits for them, and re-layouts  5 us
  transfers between devices with their start and end apart: 3, of which 2 were waited for; matrix products, arithmetic and copies ran while one was open for 4% of the time, Pallas kernels for 0%

commit v1 on v0

--- a/solution.py
+++ b/solution.py
@@ -2,6 +2,19 @@
 import jax.numpy as jnp
 from jax import lax
 from jax.sharding import PartitionSpec as P
+
+
+def gather_around(x, axis, dim):
+    ways = lax.axis_size(axis)
+    up = [(d, (d + 1) % ways) for d in range(ways)]
+    down = [(d, (d - 1) % ways) for d in range(ways)]
+    earlier, later = ([x], [x])
+    for _ in range(ways // 2):
+        earlier.append(lax.ppermute(earlier[-1], axis, up))
+    for _ in range((ways - 1) // 2):
+        later.append(lax.ppermute(later[-1], axis, down))
+    line = jnp.concatenate([*earlier[::-1], *later[1:]], axis=dim)
+    return jnp.roll(line, (lax.axis_index(axis) - ways // 2) * x.shape[dim], axis=dim)
 
 
 def body(a_blocks, block_list, block_count, w_factor, h_factor):
@@ -14,7 +27,7 @@
     tile_rows = w_tile.shape[0]
     n_row = lax.axis_size("row")
     w_rows = w_tile.reshape(row_blocks, width, rank)
-    h_all = lax.all_gather(h_factor, "row", axis=1, tiled=True)
+    h_all = gather_around(h_factor, "row", 1)
     numer_h = jnp.zeros((rank, n_row * width), jnp.float32)
     parts_w = []
     for brow in range(row_blocks):

time: 124 us -> 119 us (0.960)
  blocking collectives: 48.5 us -> 32.3 us
  starting transfers between devices: 0.12 us -> 5.29 us
  local copies, waits for them, and re-layouts: 7.19 us -> 9.44 us
  waiting for transfers between devices: 34.3 us -> 36.4 us
  matrix products: 5.36 us -> 6.65 us
    all_gather x1 -> x0, blocking collectives: 17.6 us -> none  [body(): h_all = lax.all_gather(h_factor, 'row', axis=1, tiled=True)]
    ppermute x0 -> x3, starting transfers between devices: none -> 5.17 us  [the longest x2 3.08 us: gather_around(): earlier.append(lax.ppermute(earlier[-1], axis, up))]
    ppermute x0 -> x3, waiting for transfers between devices: none -> 4.48 us  [the longest x2 4.48 us: gather_around(): earlier.append(lax.ppermute(earlier[-1], axis, up))]
    reduce_scatter x1, waiting for transfers between devices: 15.5 us -> 13.1 us  [body(): mine = lax.psum_scatter(numer_w, 'col', scatter_dimension=0, tiled=True)]
    unnamed x11 -> x26, local copies, waits for them, and re-layouts: 5 us -> 7.21 us
    psum x1, blocking collectives: 30.9 us -> 32.3 us  [body(): sums = lax.psum(sums, ('row', 'col', 'sub'))]
  transfers between devices with their start and end apart: 3 -> 6, of which waited for: 2 -> 3; matrix products, arithmetic and copies ran while one was open for 4% -> 8% of each run, Pallas kernels for 0% -> 0%
where the time goes in v1:
time: 119 us
  waiting for transfers between devices  36.4 us (31%)
  blocking collectives  32.3 us (27%)
  between operations  24.4 us (21%)
  local copies, waits for them, and re-layouts  9.44 us (8%)
  matrix products  6.65 us (6%)
  starting transfers between devices  5.29 us (4%)
  other arithmetic  4.14 us (3%)
    psum x1, blocking collectives, body(): sums = lax.psum(sums, ('row', 'col', 'sub'))  32.3 us
    psum x1, waiting for transfers between devices, body(): numer_h = lax.psum(numer_h, 'sub')  18.7 us
    reduce_scatter x1, waiting for transfers between devices, body(): mine = lax.psum_scatter(numer_w, 'col', scatter_dimension=0, tiled=True)  13.1 us
    unnamed x26, local copies, waits for them, and re-layouts  7.21 us
    ppermute x2, waiting for transfers between devices, gather_around(): earlier.append(lax.ppermute(earlier[-1], axis, up))  4.48 us
    ppermute x2, starting transfers between devices, gather_around(): earlier.append(lax.ppermute(earlier[-1], axis, up))  3.08 us
    dot_general x8, matrix products, body(): product = jnp.dot(w_rows[brow], h_block, preferred_element_type=jnp.float32)  2.68 us
    dot_general x8, matrix products, body(): jnp.einsum('ij,kj->ik', ratios, h_block, preferred_element_type=jnp.float32)  2.44 us
  transfers between devices with their start and end apart: 6, of which 3 were waited for; matrix products, arithmetic and copies ran while one was open for 8% of the time, Pallas kernels for 0%

profile of v1, /device:TPU:0, one launch (start us, length us, event | category | flops | bytes accessed | tf_op | source)
XLA Modules:
  0.0 118.6 jit_solution(9403272897273784533)
XLA Ops:
  7.2 0.0 reduce-scatter.5.cloned.1.call-start
  7.2 3.1 %collective-permute-start = (bf16[256,256]{1,0:T(8,128)(2,1)}, bf16[256,256]{1,0:T(8,128)(2,1)S(1)}, u32[]{:S(2)}, u32[]{:S(2)}) collective-permute-start(bf16[256,256]{1,0:T(8,128)(2,1)} %param.9), channel_id=1, source_target_pairs={{0,4},{4,8},{8,12},{12,0},{1,5},{5,9},{9,13},{13,1},{2,6},{6,10},{... | collective-permute-start | bytes 393224 | tf_op jit(solution)/shard_map/ppermute | solution.py:13
  10.3 2.1 %collective-permute-start.2 = (bf16[256,256]{1,0:T(8,128)(2,1)}, bf16[256,256]{1,0:T(8,128)(2,1)S(1)}, u32[]{:S(2)}, u32[]{:S(2)}) collective-permute-start(bf16[256,256]{1,0:T(8,128)(2,1)} %param.9), channel_id=1, source_target_pairs={{0,12},{4,0},{8,4},{12,8},{1,13},{5,1},{9,5},{13,9},{2,14},{6,2},{... | collective-permute-start | bytes 393224 | tf_op jit(solution)/shard_map/ppermute | solution.py:15
  12.4 4.5 %collective-permute-done = bf16[256,256]{1,0:T(8,128)(2,1)S(1)} collective-permute-done((bf16[256,256]{1,0:T(8,128)(2,1)}, bf16[256,256]{1,0:T(8,128)(2,1)S(1)}, u32[]{:S(2)}, u32[]{:S(2)}) %collective-permute-start) | collective-permute-done | bytes 131104 | tf_op jit(solution)/shard_map/ppermute | solution.py:13
  16.9 0.0 collective-permute-start.1
  16.9 1.5 %fusion.116 = (s32[1,1,1]{2,1,0:T(1,128)}, s32[1,1,1]{2,1,0:T(1,128)}, s32[1,1,1]{2,1,0:T(1,128)}, s32[1,1,1]{2,1,0:T(1,128)}) fusion(s32[1,1,4]{2,1,0:T(1,128)} %param.7), kind=kLoop, calls=%fused_computation.160 | loop fusion | bytes 32 | tf_op jit(solution)/shard_map/slice | solution.py:37
  23.4 0.0 copy-start.7
  23.4 0.7 copy-done.7
  24.1 0.7 fusion.115
  29.9 1.5 %copy.7 = bf16[1,1,4,2,256,256]{4,5,3,2,1,0:T(8,128)(2,1)S(1)} copy(bf16[1,1,4,2,256,256]{5,4,3,2,1,0:T(8,128)(2,1)} %param.5) | data formatting | bytes 2097152 | tf_op args[0]
  31.4 0.0 collective-permute-done.1
  31.4 0.0 copy-start.2
  31.4 0.9 copy-done.2
  32.3 0.0 collective-permute-done.2
  32.4 0.0 copy-start.1
  32.4 1.0 copy-done.1
  33.4 0.3 fusion.35
  33.7 0.3 fusion.36
  34.1 0.3 fusion.37
  34.4 0.3 fusion.38
  34.8 0.0 copy-start.3
  34.8 0.3 fusion.39
  35.1 0.3 fusion.40
  35.5 0.0 copy-start.5
  35.5 0.3 fusion.41
  35.8 0.3 fusion.42
  36.2 0.1 broadcast_in_dim.15
  36.2 0.2 fusion.18
  36.4 0.2 fusion.17
  36.6 0.0 copy-done.5
  36.6 0.2 fusion.15
  36.8 0.2 fusion.13
  37.1 0.2 fusion.11
  37.3 0.2 fusion.9
  37.5 0.2 fusion.7
  37.7 0.2 fusion.5
  37.9 1.0 copy-done
  38.9 0.0 reduce-scatter.5.cloned.1.call-update
  38.9 0.0 reduce-scatter.3.cloned.1.call-start
  39.0 0.3 fusion.77
  39.3 0.3 fusion.3
  39.6 0.0 copy-start.6
  39.6 0.3 fusion.72
  39.9 0.6 copy-done.6
  40.5 0.3 fusion.2
  40.8 0.0 copy-start.4
  40.8 0.3 fusion.67
  41.1 0.6 copy-done.4
  41.7 0.3 fusion.1
  42.0 0.3 fusion.62
  42.3 0.3 fusion
  42.6 1.0 pad_maximum_fusion
  43.7 0.0 reduce-scatter.3.cloned.1.call-update
  43.7 0.0 all-reduce.2.cloned.1.call-start
  43.8 0.1 copy.8
  43.9 0.1 convert_reduce_fusion.1
  43.9 0.2 convert_reduce_fusion
  44.1 32.3 %psum.14 = f32[512]{0:T(512)S(1)} all-reduce(f32[512]{0:T(512)S(1)} %pad_maximum_fusion.1), channel_id=1, replica_groups=mesh['grp'=2,'row'=4,'col'=2,'sub'=2] {'row','col','sub'}, use_global_device_ids=true, to_apply=%region_3.4 | all-reduce | flops 512 | bytes 4096 | tf_op jit(solution)/shard_map/psum | solution.py:57
  76.5 0.0 all-reduce.2.cloned.1.call-update
  76.5 13.1 %reduce-scatter.3.cloned.1.call-done = f32[512,256]{1,0:T(8,128)} async-done(((f32[1024,256]{1,0:T(8,128)}), f32[512,256]{1,0:T(8,128)}) %reduce-scatter.3.cloned.1.call-update) | async-done | bytes 524304 | tf_op jit(solution)/shard_map/reduce_scatter | solution.py:65
  89.6 1.9 %fusion.44 = f32[1,512,256]{2,1,0:T(8,128)} fusion(f32[512,256]{1,0:T(8,128)} %reduce-scatter.3.cloned.1.call-done, f32[256]{0:T(256)S(1)} %get-tuple-element.5, bf16[1,1024,256]{2,1,0:T(8,128)(2,1)S(1)} %copy-done.1, s32[]{:T(128)S(6)} %select_n.137), kind=kLoop, calls=%fused_computation.67 | loop fusion | flops 393216 | bytes 1311748 | tf_op jit(solution)/shard_map/broadcast_in_dim | solution.py:67
  91.5 18.7 %all-reduce.2.cloned.1.call-done = f32[256,256]{0,1:T(8,128)} async-done(((f32[256,256]{0,1:T(8,128)}), f32[256,256]{0,1:T(8,128)}) %all-reduce.2.cloned.1.call-update) | async-done | bytes 262160 | tf_op jit(solution)/shard_map/psum | solution.py:61
  110.2 1.0 fusion.45
  111.2 0.8 copy.9
  (15 shorter events, 0.1 us)
Async XLA Ops:
  7.2 69.3 %reduce-scatter.5.cloned.1.call-start = ((), (), s32[]{:S(2)}) async-start(), calls=%async_computation.3 | async-start | bytes 1310720 | tf_op jit(solution)/shard_map/reduce_scatter | solution.py:60
  7.2 9.6 %collective-permute-start = (bf16[256,256]{1,0:T(8,128)(2,1)}, bf16[256,256]{1,0:T(8,128)(2,1)S(1)}, u32[]{:S(2)}, u32[]{:S(2)}) collective-permute-start(bf16[256,256]{1,0:T(8,128)(2,1)} %param.9), channel_id=1, source_target_pairs={{0,4},{4,8},{8,12},{12,0},{1,5},{5,9},{9,13},{13,1},{2,6},{6,10},{... | collective-permute-start | bytes 393224 | tf_op jit(solution)/shard_map/ppermute | solution.py:13
  10.3 22.0 %collective-permute-start.2 = (bf16[256,256]{1,0:T(8,128)(2,1)}, bf16[256,256]{1,0:T(8,128)(2,1)S(1)}, u32[]{:S(2)}, u32[]{:S(2)}) collective-permute-start(bf16[256,256]{1,0:T(8,128)(2,1)} %param.9), channel_id=1, source_target_pairs={{0,12},{4,0},{8,4},{12,8},{1,13},{5,1},{9,5},{13,9},{2,14},{6,2},{... | collective-permute-start | bytes 393224 | tf_op jit(solution)/shard_map/ppermute | solution.py:15
  16.9 14.5 %collective-permute-start.1 = (bf16[256,256]{1,0:T(8,128)(2,1)S(1)}, bf16[256,256]{1,0:T(8,128)(2,1)S(1)}, u32[]{:S(2)}, u32[]{:S(2)}) collective-permute-start(bf16[256,256]{1,0:T(8,128)(2,1)S(1)} %collective-permute-done), channel_id=1, source_target_pairs={{0,4},{4,8},{8,12},{12,0},{1,5},{5,9},{9,13},{13,1},{2,6},{6,10},{... | collective-permute-start | bytes 393224 | tf_op jit(solution)/shard_map/ppermute | solution.py:13
  23.4 0.7 copy-start.7
  31.4 0.9 copy-start.2
  32.4 1.0 copy-start.1
  34.8 2.3 %copy-start.3 = (bf16[256,256]{0,1:T(8,128)(2,1)}, bf16[256,256]{0,1:T(8,128)(2,1)S(1)}, u32[]{:S(2)}) copy-start(bf16[256,256]{0,1:T(8,128)(2,1)S(1)} %fusion.38) | copy-start | bytes 393220
  35.5 1.2 copy-start.5
  37.9 1.0 copy-start
  38.9 50.7 %reduce-scatter.3.cloned.1.call-start = ((), (), s32[]{:S(2)}) async-start(), calls=%async_computation.2 | async-start | bytes 1572864 | tf_op jit(solution)/shard_map/reduce_scatter | solution.py:65
  39.6 0.9 copy-start.6
  40.8 0.9 copy-start.4
  43.7 66.5 %all-reduce.2.cloned.1.call-start = ((), (), s32[]{:S(2)}) async-start(), calls=%async_computation.4 | async-start | bytes 524288 | tf_op jit(solution)/shard_map/psum | solution.py:61
Sparse Core Ops, SparseCore 0:
  39.0 29.1 reduce-scatter.4
  70.5 19.0 reduce-scatter.2
  91.9 18.2 all-reduce.1
